TPU v7x, 256 devices: a whole 4x4x8 slice. The times are simulated.
256 devices in a mesh: ctx: 32 (over z, x), tp: 8 (over y, core).
Axes of the slice: x: 4, y: 4, z: 8, core: 2. Of those that a mesh axis runs over, the one named last changes fastest.
Arguments:
- tokens: bfloat16 [16384, 3072], P(('ctx', 'tp')), may hold values from -6 to 6
- w_query: bfloat16 [3072, 4096], P(None, 'tp'), may hold values from -0.109375 to 0.109375
- w_key: bfloat16 [3072, 4096], P(None, 'tp'), may hold values from -0.109375 to 0.109375
- w_value: bfloat16 [3072, 4096], P(None, 'tp'), may hold values from -0.109375 to 0.109375
- norm_gain: float32 [4096], P('tp'), may hold values from 0.1 to 1.9
Outputs:
- attended: bfloat16 [16384, 4096], P('ctx', 'tp')
All inputs are finite; a program needn't handle non-finite values.
Results may differ from a plain program's by a relative error of at most 0.0062.
Values may be sent and summed in bfloat16 or wider, within the bound.
No kernel may reach another device: no remote copies, remote signals or barrier semaphores. Data moves between devices by JAX's collectives and lax.ppermute only.
A program may use at most 64 MiB of HBM per device.

v0:
```python
import jax
import jax.numpy as jnp
from jax import lax
from jax.sharding import PartitionSpec as P

HEAD_DIM = 128
BLOCK = 512
EPSILON = 1e-06


def from_behind(value, axis, by):
    size = lax.axis_size(axis)
    pairs = [(i, i + by) for i in range(size) if 0 <= i + by < size]
    return lax.ppermute(value, axis, pairs)


def exclusive_scan(value, axis):
    size = lax.axis_size(axis)
    covered = value
    before = None
    by = 1
    while by < size:
        piece = from_behind(covered, axis, by)
        before = piece if before is None else before + piece
        by *= 2
        if by < size:
            covered = covered + piece
    return before


def body(tokens, w_query, w_key, w_value, norm_gain):
    local_width = w_query.shape[1]
    head_count = local_width // HEAD_DIM
    piece_rows = lax.all_gather(tokens, "tp", axis=0, tiled=True)
    query_part = jnp.dot(piece_rows, w_query, preferred_element_type=jnp.float32).astype(
        jnp.bfloat16
    )
    key_part = jnp.dot(piece_rows, w_key, preferred_element_type=jnp.float32).astype(jnp.bfloat16)
    value_part = jnp.dot(piece_rows, w_value, preferred_element_type=jnp.float32).astype(
        jnp.bfloat16
    )
    projected = jnp.concatenate([query_part, key_part, value_part], axis=1)
    group_len = projected.shape[0]
    block_count = group_len // BLOCK
    shaped = projected.reshape(block_count, BLOCK, 3, head_count, HEAD_DIM)
    query_rows = shaped[:, :, 0]
    key_rows = shaped[:, :, 1]
    value_rows = shaped[:, :, 2]
    block_states = jnp.einsum(
        "bshd,bshe->bhde", key_rows, value_rows, preferred_element_type=jnp.float32
    )
    local_state = jnp.sum(block_states, axis=0)
    prefix_state = exclusive_scan(local_state, "ctx")
    running = jnp.cumsum(block_states, axis=0)
    earlier = jnp.concatenate([jnp.zeros_like(block_states), running[:-1]], axis=0)
    block_start = prefix_state[None] + earlier
    scores = jnp.einsum("bqhd,bkhd->bhqk", query_rows, key_rows, preferred_element_type=jnp.float32)
    causal = jnp.arange(BLOCK)[:, None] >= jnp.arange(BLOCK)[None, :]
    scores = jnp.where(causal[None, None], scores, jnp.float32(0.0)).astype(jnp.bfloat16)
    inner = jnp.einsum("bhqk,bkhe->bqhe", scores, value_rows, preferred_element_type=jnp.float32)
    carried_part = jnp.einsum(
        "bqhd,bhde->bqhe",
        query_rows.astype(jnp.float32),
        block_start,
        precision=lax.Precision.HIGHEST,
    )
    mixed = inner + carried_part
    mean_square = jnp.mean(mixed * mixed, axis=-1, keepdims=True)
    normed = mixed * lax.rsqrt(mean_square + EPSILON) * norm_gain.reshape(head_count, HEAD_DIM)
    return normed.reshape(group_len, local_width).astype(jnp.bfloat16)


def solution(mesh):
    placed = (P(("ctx", "tp"), None), P(None, "tp"), P(None, "tp"), P(None, "tp"), P("tp"))
    return jax.shard_map(
        body, mesh=mesh, in_specs=placed, out_specs=P("ctx", "tp"), check_vma=False
    )
```

profile of v0, /device:TPU:192, one launch (start us, length us, event | category | flops | bytes accessed | tf_op | source)
XLA Modules:
  0.0 132.0 jit_solution(15375087548146200491)
XLA Ops:
  6.5 0.0 copy-start
  6.5 0.0 all-gather.2.cloned.1.call-start
  6.5 0.7 all-gather.2.cloned.1.call-update
  7.3 33.0 %all-gather.2.cloned.1.call-done = bf16[512,3072]{1,0:T(8,128)(2,1)} async-done(((bf16[64,3072]{1,0:T(8,128)(2,1)}), bf16[512,3072]{1,0:T(8,128)(2,1)}) %all-gather.2.cloned.1.call-update) | async-done | bytes 3145744 | tf_op jit(solution)/shard_map/all_gather | solution.py:34
  40.3 0.0 copy-done
  40.3 0.0 copy-start.6
  40.3 0.0 copy-start.8
  40.3 3.9 %convolution_convert_fusion = bf16[512,512]{0,1:T(8,128)(2,1)S(1)} fusion(bf16[512,3072]{1,0:T(8,128)(2,1)} %all-gather.2.cloned.1.call-done, bf16[3072,512]{1,0:T(8,128)(2,1)S(1)} %copy-done), kind=kOutput, calls=%fused_computation.5 | convolution fusion | flops 1610874880 | bytes 6815744 | tf_op jit(solution)/shard_map/dot_general | solution.py:39
  44.1 0.0 copy-done.6
  44.1 0.0 copy-done.8
  44.2 0.0 copy-start.7
  44.2 1.8 %convolution_convert_fusion.1 = bf16[512,512]{0,1:T(8,128)(2,1)S(1)} fusion(bf16[512,3072]{1,0:T(8,128)(2,1)S(1)} %copy-done.8, bf16[3072,512]{1,0:T(8,128)(2,1)S(1)} %copy-done.6), kind=kOutput, calls=%fused_computation.6 | convolution fusion | flops 1610874880 | bytes 6815744 | tf_op jit(solution)/shard_map/dot_general | solution.py:38
  46.0 0.0 copy-done.7
  46.1 1.8 %convolution_convert_fusion.2 = bf16[512,512]{0,1:T(8,128)(2,1)S(1)} fusion(bf16[512,3072]{1,0:T(8,128)(2,1)S(1)} %copy-done.8, bf16[3072,512]{1,0:T(8,128)(2,1)S(1)} %copy-done.7), kind=kOutput, calls=%fused_computation.7 | convolution fusion | flops 1610874880 | bytes 6815744 | tf_op jit(solution)/shard_map/dot_general | solution.py:35
  47.9 0.1 pad_maximum_fusion
  48.0 0.0 copy-start.1
  48.0 1.2 copy-done.1
  49.2 0.3 fusion.2
  49.5 3.4 %collective-permute-start = (f32[4,128,128]{2,1,0:T(8,128)S(1)}, f32[4,128,128]{2,1,0:T(8,128)S(1)}, u32[]{:S(2)}, u32[]{:S(2)}) collective-permute-start(f32[4,128,128]{2,1,0:T(8,128)S(1)} %fusion.2), channel_id=1, source_target_pairs={{0,8},{8,16},{16,24},{24,32},{32,40},{40,48},{48,56},{56,64},{64,7... | collective-permute-start | bytes 786440 | tf_op jit(solution)/shard_map/ppermute | solution.py:14
  52.8 9.1 %collective-permute-done = f32[4,128,128]{2,1,0:T(8,128)S(1)} collective-permute-done((f32[4,128,128]{2,1,0:T(8,128)S(1)}, f32[4,128,128]{2,1,0:T(8,128)S(1)}, u32[]{:S(2)}, u32[]{:S(2)}) %collective-permute-start) | collective-permute-done | bytes 262176 | tf_op jit(solution)/shard_map/ppermute | solution.py:14
  61.9 2.8 %collective-permute-start.1 = (f32[4,128,128]{2,1,0:T(8,128)S(1)}, f32[4,128,128]{2,1,0:T(8,128)S(1)}, u32[]{:S(2)}, u32[]{:S(2)}) collective-permute-start(f32[4,128,128]{2,1,0:T(8,128)S(1)} %add.44), channel_id=1, source_target_pairs={{0,16},{8,24},{16,32},{24,40},{32,48},{40,56},{48,64},{56,72},{64,... | collective-permute-start | bytes 786440 | tf_op jit(solution)/shard_map/ppermute | solution.py:14
  64.7 9.1 %collective-permute-done.1 = f32[4,128,128]{2,1,0:T(8,128)S(1)} collective-permute-done((f32[4,128,128]{2,1,0:T(8,128)S(1)}, f32[4,128,128]{2,1,0:T(8,128)S(1)}, u32[]{:S(2)}, u32[]{:S(2)}) %collective-permute-start.1) | collective-permute-done | bytes 262176 | tf_op jit(solution)/shard_map/ppermute | solution.py:14
  73.8 0.0 copy-start.2
  73.9 2.6 %collective-permute-start.2 = (f32[4,128,128]{2,1,0:T(8,128)S(1)}, f32[4,128,128]{2,1,0:T(8,128)S(1)}, u32[]{:S(2)}, u32[]{:S(2)}) collective-permute-start(f32[4,128,128]{2,1,0:T(8,128)S(1)} %add.46), channel_id=1, source_target_pairs={{0,32},{8,40},{16,48},{24,56},{32,64},{40,72},{48,80},{56,88},{64,... | collective-permute-start | bytes 786440 | tf_op jit(solution)/shard_map/ppermute | solution.py:14
  76.4 6.1 %collective-permute-done.2 = f32[4,128,128]{2,1,0:T(8,128)S(1)} collective-permute-done((f32[4,128,128]{2,1,0:T(8,128)S(1)}, f32[4,128,128]{2,1,0:T(8,128)S(1)}, u32[]{:S(2)}, u32[]{:S(2)}) %collective-permute-start.2) | collective-permute-done | bytes 262176 | tf_op jit(solution)/shard_map/ppermute | solution.py:14
  82.5 0.0 copy-start.3
  82.5 1.3 collective-permute-start.3
  83.8 0.8 iota_compare_fusion
  84.6 15.5 %collective-permute-done.3 = f32[4,128,128]{2,1,0:T(8,128)S(1)} collective-permute-done((f32[4,128,128]{2,1,0:T(8,128)S(1)}, f32[4,128,128]{2,1,0:T(8,128)S(1)}, u32[]{:S(2)}, u32[]{:S(2)}) %collective-permute-start.3) | collective-permute-done | bytes 262176 | tf_op jit(solution)/shard_map/ppermute | solution.py:14
  100.1 0.0 copy-start.4
  100.1 0.8 add.50
  100.9 0.0 copy-done.2
  100.9 0.0 copy-done.3
  100.9 0.0 copy-done.4
  100.9 1.3 collective-permute-start.4
  102.2 3.8 %fusion = f32[4,128,512]{2,1,0:T(8,128)} fusion(pred[512,512]{1,0:T(8,128)(4,1)} %iota_compare_fusion, bf16[1,512,3,4,128]{1,4,3,2,0:T(8,128)(2,1)} %bitcast.30), kind=kOutput, calls=%fused_computation.1 | convolution fusion | flops 538968064 | bytes 2883584 | tf_op jit(solution)/shard_map/bhqk,bkhe->bqhe/dot_general | solution.py:60
  106.0 0.0 copy-start.5
  106.0 13.7 %collective-permute-done.4 = f32[4,128,128]{2,1,0:T(8,128)} collective-permute-done((f32[4,128,128]{2,1,0:T(8,128)}, f32[4,128,128]{2,1,0:T(8,128)}, u32[]{:S(2)}, u32[]{:S(2)}) %collective-permute-start.4) | collective-permute-done | bytes 262176 | tf_op jit(solution)/shard_map/ppermute | solution.py:14
  119.7 2.4 %multiply_reduce_fusion = (f32[512,4]{0,1:T(4,128)S(1)}, f32[1,512,4,128]{1,3,2,0:T(8,128)S(1)}) fusion(f32[4,128,512]{2,1,0:T(8,128)} %fusion, bf16[1,512,3,4,128]{1,4,3,2,0:T(8,128)(2,1)} %bitcast.31, f32[4,128,128]{2,1,0:T(8,128)} %collective-permute-done.4, f32[4,128,128]{2,1,0:T(8,128)} %copy-done.4, f32[4,128,128]{2,1,0:T(8,128)} %copy-done.3, ...), kind=kOutput, calls=%fused_computation.9 | convolution fusion | flops 403699712 | bytes 3940352 | tf_op jit(solution)/shard_map/bqhd,bhde->bqhe/dot_general | solution.py:61
  122.1 0.0 copy-done.5
  122.1 0.9 multiply_convert_fusion
  123.1 2.0 %copy.9 = bf16[512,512]{1,0:T(8,128)(2,1)} copy(bf16[512,512]{0,1:T(8,128)(2,1)} %bitcast.32) | data formatting | bytes 1048576 | tf_op jit(solution)/shard_map/convert_element_type | solution.py:70
  (4 shorter events, 0.1 us)
Async XLA Ops:
  6.5 33.7 %copy-start = (bf16[3072,512]{1,0:T(8,128)(2,1)S(1)}, bf16[3072,512]{1,0:T(8,128)(2,1)}, u32[]{:S(2)}) copy-start(bf16[3072,512]{1,0:T(8,128)(2,1)} %param.8) | copy-start | bytes 9437188
  6.5 33.7 %all-gather.2.cloned.1.call-start = ((), (), s32[]{:S(2)}) async-start(), calls=%async_computation | async-start | bytes 3538944 | tf_op jit(solution)/shard_map/all_gather | solution.py:34
  40.3 3.9 %copy-start.6 = (bf16[3072,512]{1,0:T(8,128)(2,1)S(1)}, bf16[3072,512]{1,0:T(8,128)(2,1)}, u32[]{:S(2)}) copy-start(bf16[3072,512]{1,0:T(8,128)(2,1)} %param.7) | copy-start | bytes 9437188
  40.3 3.9 %copy-start.8 = (bf16[512,3072]{1,0:T(8,128)(2,1)S(1)}, bf16[512,3072]{1,0:T(8,128)(2,1)}, u32[]{:S(2)}) copy-start(bf16[512,3072]{1,0:T(8,128)(2,1)} %all-gather.2.cloned.1.call-done) | copy-start | bytes 9437188
  44.2 1.9 %copy-start.7 = (bf16[3072,512]{1,0:T(8,128)(2,1)S(1)}, bf16[3072,512]{1,0:T(8,128)(2,1)}, u32[]{:S(2)}) copy-start(bf16[3072,512]{1,0:T(8,128)(2,1)} %param.6) | copy-start | bytes 9437188
  48.0 1.2 copy-start.1
  49.5 12.5 %collective-permute-start = (f32[4,128,128]{2,1,0:T(8,128)S(1)}, f32[4,128,128]{2,1,0:T(8,128)S(1)}, u32[]{:S(2)}, u32[]{:S(2)}) collective-permute-start(f32[4,128,128]{2,1,0:T(8,128)S(1)} %fusion.2), channel_id=1, source_target_pairs={{0,8},{8,16},{16,24},{24,32},{32,40},{40,48},{48,56},{56,64},{64,7... | collective-permute-start | bytes 786440 | tf_op jit(solution)/shard_map/ppermute | solution.py:14
  61.9 11.9 %collective-permute-start.1 = (f32[4,128,128]{2,1,0:T(8,128)S(1)}, f32[4,128,128]{2,1,0:T(8,128)S(1)}, u32[]{:S(2)}, u32[]{:S(2)}) collective-permute-start(f32[4,128,128]{2,1,0:T(8,128)S(1)} %add.44), channel_id=1, source_target_pairs={{0,16},{8,24},{16,32},{24,40},{32,48},{40,56},{48,64},{56,72},{64,... | collective-permute-start | bytes 786440 | tf_op jit(solution)/shard_map/ppermute | solution.py:14
  73.8 27.1 %copy-start.2 = (f32[4,128,128]{2,1,0:T(8,128)}, f32[4,128,128]{2,1,0:T(8,128)S(1)}, u32[]{:S(2)}) copy-start(f32[4,128,128]{2,1,0:T(8,128)S(1)} %collective-permute-done.1) | copy-start | bytes 786436
  73.9 8.6 %collective-permute-start.2 = (f32[4,128,128]{2,1,0:T(8,128)S(1)}, f32[4,128,128]{2,1,0:T(8,128)S(1)}, u32[]{:S(2)}, u32[]{:S(2)}) collective-permute-start(f32[4,128,128]{2,1,0:T(8,128)S(1)} %add.46), channel_id=1, source_target_pairs={{0,32},{8,40},{16,48},{24,56},{32,64},{40,72},{48,80},{56,88},{64,... | collective-permute-start | bytes 786440 | tf_op jit(solution)/shard_map/ppermute | solution.py:14
  82.5 18.4 %copy-start.3 = (f32[4,128,128]{2,1,0:T(8,128)}, f32[4,128,128]{2,1,0:T(8,128)S(1)}, u32[]{:S(2)}) copy-start(f32[4,128,128]{2,1,0:T(8,128)S(1)} %collective-permute-done.2) | copy-start | bytes 786436
  82.5 17.6 %collective-permute-start.3 = (f32[4,128,128]{2,1,0:T(8,128)S(1)}, f32[4,128,128]{2,1,0:T(8,128)S(1)}, u32[]{:S(2)}, u32[]{:S(2)}) collective-permute-start(f32[4,128,128]{2,1,0:T(8,128)S(1)} %add.48), channel_id=1, source_target_pairs={{0,64},{8,72},{16,80},{24,88},{32,96},{40,104},{48,112},{56,120},{... | collective-permute-start | bytes 786440 | tf_op jit(solution)/shard_map/ppermute | solution.py:14
  100.1 0.8 copy-start.4
  100.9 18.8 %collective-permute-start.4 = (f32[4,128,128]{2,1,0:T(8,128)}, f32[4,128,128]{2,1,0:T(8,128)}, u32[]{:S(2)}, u32[]{:S(2)}) collective-permute-start(f32[4,128,128]{2,1,0:T(8,128)} %add.50), channel_id=1, source_target_pairs={{0,128},{8,136},{16,144},{24,152},{32,160},{40,168},{48,176},{56,1... | collective-permute-start | bytes 786440 | tf_op jit(solution)/shard_map/ppermute | solution.py:14
  106.0 16.1 %copy-start.5 = (f32[512]{0:T(512)S(1)}, f32[512]{0:T(512)}, u32[]{:S(2)}) copy-start(f32[512]{0:T(512)} %param.9) | copy-start | bytes 6148
Sparse Core Ops, SparseCore 0:
  9.2 31.0 all-gather.1
where the time goes:
time: 132 us
  waiting for transfers between devices  87.1 us (66%)
  matrix products  14 us (11%)
  between operations  13.5 us (10%)
  starting transfers between devices  11.3 us (9%)
  local copies, waits for them, and re-layouts  3.27 us (2%)
  other arithmetic  2.72 us (2%)
    ppermute x5, waiting for transfers between devices, from_behind(): return lax.ppermute(value, axis, pairs)  53.4 us
    all_gather x1, waiting for transfers between devices, body(): piece_rows = lax.all_gather(tokens, 'tp', axis=0, tiled=True)  33 us
    ppermute x5, starting transfers between devices, from_behind(): return lax.ppermute(value, axis, pairs)  11.3 us
    dot_general x1, matrix products, body(): jnp.dot(piece_rows, w_value, preferred_element_type=jnp.float32)  3.87 us
    dot_general x1, matrix products, body(): jnp.einsum('bhqk,bkhe->bqhe', scores, value_rows, preferred_element_type=...  3.8 us
  transfers between devices with their start and end apart: 6, of which 6 were waited for; matrix products, arithmetic and copies ran while one was open for 3% of the time, Pallas kernels for 0%

commit v1 on v0

--- a/solution.py
+++ b/solution.py
@@ -31,7 +31,9 @@
 def body(tokens, w_query, w_key, w_value, norm_gain):
     local_width = w_query.shape[1]
     head_count = local_width // HEAD_DIM
-    piece_rows = lax.all_gather(tokens, "tp", axis=0, tiled=True)
+    piece_rows = jnp.concatenate(
+        lax.all_to_all(jnp.stack([tokens] * lax.axis_size("tp")), "tp", 0, 0), axis=0
+    )
     query_part = jnp.dot(piece_rows, w_query, preferred_element_type=jnp.float32).astype(
         jnp.bfloat16
     )

time: 132 us -> 123 us (0.932)
  blocking collectives: 0 us -> 42.7 us
  waiting for transfers between devices: 87.1 us -> 48.9 us
  between operations: 13.5 us -> 0.14 us
  matrix products: 14 us -> 12 us
  local copies, waits for them, and re-layouts: 3.27 us -> 4.8 us
    all_to_all x0 -> x1, blocking collectives: none -> 42.7 us  [body(): lax.all_to_all(jnp.stack([tokens] * lax.axis_size('tp')), 'tp', 0, 0)]
    all_gather x1 -> x0, waiting for transfers between devices: 33 us -> none  [body(): piece_rows = lax.all_gather(tokens, 'tp', axis=0, tiled=True)]
    ppermute x5, waiting for transfers between devices: 53.4 us -> 48.9 us  [from_behind(): return lax.ppermute(value, axis, pairs)]
    dot_general x1, matrix products: 3.87 us -> 1.86 us  [body(): jnp.dot(piece_rows, w_value, preferred_element_type=jnp.float32)]
    another operation x0 -> x1, local copies, waits for them, and re-layouts: none -> 1.51 us  [body(): jnp.stack([tokens] * lax.axis_size('tp'))]
  transfers between devices with their start and end apart: 6 -> 5, of which waited for: 6 -> 5; matrix products, arithmetic and copies ran while one was open for 3% -> 4% of each run, Pallas kernels for 0% -> 0%
where the time goes in v1:
time: 123 us
  waiting for transfers between devices  48.9 us (40%)
  blocking collectives  42.7 us (35%)
  matrix products  12 us (10%)
  starting transfers between devices  11.7 us (10%)
  local copies, waits for them, and re-layouts  4.8 us (4%)
  other arithmetic  2.71 us (2%)
    ppermute x5, waiting for transfers between devices, from_behind(): return lax.ppermute(value, axis, pairs)  48.9 us
    all_to_all x1, blocking collectives, body(): lax.all_to_all(jnp.stack([tokens] * lax.axis_size('tp')), 'tp', 0, 0)  42.7 us
    ppermute x5, starting transfers between devices, from_behind(): return lax.ppermute(value, axis, pairs)  11.7 us
    dot_general x1, matrix products, body(): jnp.einsum('bhqk,bkhe->bqhe', scores, value_rows, preferred_element_type=...  3.79 us
  transfers between devices with their start and end apart: 5, of which 5 were waited for; matrix products, arithmetic and copies ran while one was open for 4% of the time, Pallas kernels for 0%

profile of v1, /device:TPU:192, one launch (start us, length us, event | category | flops | bytes accessed | tf_op | source)
XLA Modules:
  0.0 123.0 jit_solution(2548392086073541811)
XLA Ops:
  0.0 0.0 copy-start
  0.0 1.5 %stack.2 = bf16[8,64,3072]{2,1,0:T(8,128)(2,1)S(1)} broadcast(bf16[64,3072]{1,0:T(8,128)(2,1)} %param.5), dimensions={1,2} | broadcast | bytes 3538944 | tf_op jit(solution)/shard_map/stack | solution.py:35
  1.5 42.7 %all_to_all.5 = bf16[8,64,3072]{2,1,0:T(8,128)(2,1)S(1)} all-to-all(bf16[8,64,3072]{2,1,0:T(8,128)(2,1)S(1)} %stack.2), channel_id=1, replica_groups=mesh['ctx'=32,'tp'=8] {'tp'}, dimensions={0} | all-to-all | bytes 6291456 | tf_op jit(solution)/shard_map/all_to_all | solution.py:35
  44.2 0.0 copy-done
  44.2 0.0 copy-start.6
  44.2 1.9 %convolution_convert_fusion = bf16[512,512]{0,1:T(8,128)(2,1)S(1)} fusion(bf16[512,3072]{1,0:T(8,128)(2,1)S(1)} %bitcast.30, bf16[3072,512]{1,0:T(8,128)(2,1)S(1)} %copy-done), kind=kOutput, calls=%fused_computation.5 | convolution fusion | flops 1610874880 | bytes 6815744 | tf_op jit(solution)/shard_map/dot_general | solution.py:41
  46.1 0.0 copy-done.6
  46.1 0.0 copy-start.7
  46.1 1.8 %convolution_convert_fusion.1 = bf16[512,512]{0,1:T(8,128)(2,1)S(1)} fusion(bf16[512,3072]{1,0:T(8,128)(2,1)S(1)} %bitcast.31, bf16[3072,512]{1,0:T(8,128)(2,1)S(1)} %copy-done.6), kind=kOutput, calls=%fused_computation.6 | convolution fusion | flops 1610874880 | bytes 6815744 | tf_op jit(solution)/shard_map/dot_general | solution.py:40
  48.0 0.1 copy-done.7
  48.0 1.8 %convolution_convert_fusion.2 = bf16[512,512]{0,1:T(8,128)(2,1)S(1)} fusion(bf16[512,3072]{1,0:T(8,128)(2,1)S(1)} %bitcast.32, bf16[3072,512]{1,0:T(8,128)(2,1)S(1)} %copy-done.7), kind=kOutput, calls=%fused_computation.7 | convolution fusion | flops 1610874880 | bytes 6815744 | tf_op jit(solution)/shard_map/dot_general | solution.py:37
  49.9 0.1 pad_maximum_fusion
  50.0 0.0 copy-start.1
  50.0 1.1 copy-done.1
  51.1 0.3 fusion.2
  51.4 3.4 %collective-permute-start = (f32[4,128,128]{2,1,0:T(8,128)S(1)}, f32[4,128,128]{2,1,0:T(8,128)S(1)}, u32[]{:S(2)}, u32[]{:S(2)}) collective-permute-start(f32[4,128,128]{2,1,0:T(8,128)S(1)} %fusion.2), channel_id=1, source_target_pairs={{0,8},{8,16},{16,24},{24,32},{32,40},{40,48},{48,56},{56,64},{64,7... | collective-permute-start | bytes 786440 | tf_op jit(solution)/shard_map/ppermute | solution.py:14
  54.8 8.3 %collective-permute-done = f32[4,128,128]{2,1,0:T(8,128)S(1)} collective-permute-done((f32[4,128,128]{2,1,0:T(8,128)S(1)}, f32[4,128,128]{2,1,0:T(8,128)S(1)}, u32[]{:S(2)}, u32[]{:S(2)}) %collective-permute-start) | collective-permute-done | bytes 262176 | tf_op jit(solution)/shard_map/ppermute | solution.py:14
  63.1 2.8 %collective-permute-start.1 = (f32[4,128,128]{2,1,0:T(8,128)S(1)}, f32[4,128,128]{2,1,0:T(8,128)S(1)}, u32[]{:S(2)}, u32[]{:S(2)}) collective-permute-start(f32[4,128,128]{2,1,0:T(8,128)S(1)} %add.44), channel_id=1, source_target_pairs={{0,16},{8,24},{16,32},{24,40},{32,48},{40,56},{48,64},{56,72},{64,... | collective-permute-start | bytes 786440 | tf_op jit(solution)/shard_map/ppermute | solution.py:14
  66.0 8.3 %collective-permute-done.1 = f32[4,128,128]{2,1,0:T(8,128)S(1)} collective-permute-done((f32[4,128,128]{2,1,0:T(8,128)S(1)}, f32[4,128,128]{2,1,0:T(8,128)S(1)}, u32[]{:S(2)}, u32[]{:S(2)}) %collective-permute-start.1) | collective-permute-done | bytes 262176 | tf_op jit(solution)/shard_map/ppermute | solution.py:14
  74.3 0.0 copy-start.2
  74.3 2.9 %collective-permute-start.2 = (f32[4,128,128]{2,1,0:T(8,128)S(1)}, f32[4,128,128]{2,1,0:T(8,128)S(1)}, u32[]{:S(2)}, u32[]{:S(2)}) collective-permute-start(f32[4,128,128]{2,1,0:T(8,128)S(1)} %add.46), channel_id=1, source_target_pairs={{0,32},{8,40},{16,48},{24,56},{32,64},{40,72},{48,80},{56,88},{64,... | collective-permute-start | bytes 786440 | tf_op jit(solution)/shard_map/ppermute | solution.py:14
  77.2 5.3 %collective-permute-done.2 = f32[4,128,128]{2,1,0:T(8,128)S(1)} collective-permute-done((f32[4,128,128]{2,1,0:T(8,128)S(1)}, f32[4,128,128]{2,1,0:T(8,128)S(1)}, u32[]{:S(2)}, u32[]{:S(2)}) %collective-permute-start.2) | collective-permute-done | bytes 262176 | tf_op jit(solution)/shard_map/ppermute | solution.py:14
  82.6 0.0 copy-start.3
  82.6 1.3 %collective-permute-start.3 = (f32[4,128,128]{2,1,0:T(8,128)S(1)}, f32[4,128,128]{2,1,0:T(8,128)S(1)}, u32[]{:S(2)}, u32[]{:S(2)}) collective-permute-start(f32[4,128,128]{2,1,0:T(8,128)S(1)} %add.48), channel_id=1, source_target_pairs={{0,64},{8,72},{16,80},{24,88},{32,96},{40,104},{48,112},{56,120},{... | collective-permute-start | bytes 786440 | tf_op jit(solution)/shard_map/ppermute | solution.py:14
  83.9 0.8 iota_compare_fusion
  84.7 13.7 %collective-permute-done.3 = f32[4,128,128]{2,1,0:T(8,128)S(1)} collective-permute-done((f32[4,128,128]{2,1,0:T(8,128)S(1)}, f32[4,128,128]{2,1,0:T(8,128)S(1)}, u32[]{:S(2)}, u32[]{:S(2)}) %collective-permute-start.3) | collective-permute-done | bytes 262176 | tf_op jit(solution)/shard_map/ppermute | solution.py:14
  98.3 0.0 copy-start.4
  98.3 0.8 add.50
  99.1 0.0 copy-done.2
  99.1 0.0 copy-done.3
  99.1 0.0 copy-done.4
  99.1 1.3 %collective-permute-start.4 = (f32[4,128,128]{2,1,0:T(8,128)}, f32[4,128,128]{2,1,0:T(8,128)}, u32[]{:S(2)}, u32[]{:S(2)}) collective-permute-start(f32[4,128,128]{2,1,0:T(8,128)} %add.50), channel_id=1, source_target_pairs={{0,128},{8,136},{16,144},{24,152},{32,160},{40,168},{48,176},{56,1... | collective-permute-start | bytes 786440 | tf_op jit(solution)/shard_map/ppermute | solution.py:14
  100.4 3.8 %fusion = f32[4,128,512]{2,1,0:T(8,128)} fusion(pred[512,512]{1,0:T(8,128)(4,1)} %iota_compare_fusion, bf16[1,512,3,4,128]{1,4,3,2,0:T(8,128)(2,1)} %bitcast.34), kind=kOutput, calls=%fused_computation.1 | convolution fusion | flops 538968064 | bytes 2883584 | tf_op jit(solution)/shard_map/bhqk,bkhe->bqhe/dot_general | solution.py:62
  104.2 0.0 copy-start.5
  104.2 13.3 %collective-permute-done.4 = f32[4,128,128]{2,1,0:T(8,128)} collective-permute-done((f32[4,128,128]{2,1,0:T(8,128)}, f32[4,128,128]{2,1,0:T(8,128)}, u32[]{:S(2)}, u32[]{:S(2)}) %collective-permute-start.4) | collective-permute-done | bytes 262176 | tf_op jit(solution)/shard_map/ppermute | solution.py:14
  117.5 2.4 %multiply_reduce_fusion = (f32[512,4]{0,1:T(4,128)S(1)}, f32[1,512,4,128]{1,3,2,0:T(8,128)S(1)}) fusion(f32[4,128,512]{2,1,0:T(8,128)} %fusion, bf16[1,512,3,4,128]{1,4,3,2,0:T(8,128)(2,1)} %bitcast.35, f32[4,128,128]{2,1,0:T(8,128)} %collective-permute-done.4, f32[4,128,128]{2,1,0:T(8,128)} %copy-done.4, f32[4,128,128]{2,1,0:T(8,128)} %copy-done.3, ...), kind=kOutput, calls=%fused_computation.9 | convolution fusion | flops 403699712 | bytes 3940352 | tf_op jit(solution)/shard_map/bqhd,bhde->bqhe/dot_general | solution.py:63
  120.0 0.0 copy-done.5
  120.0 0.9 multiply_convert_fusion
  120.9 2.0 %copy.9 = bf16[512,512]{1,0:T(8,128)(2,1)} copy(bf16[512,512]{0,1:T(8,128)(2,1)} %bitcast.36) | data formatting | bytes 1048576 | tf_op jit(solution)/shard_map/convert_element_type | solution.py:72
  (4 shorter events, 0.1 us)
Async XLA Ops:
  0.0 44.2 %copy-start = (bf16[3072,512]{1,0:T(8,128)(2,1)S(1)}, bf16[3072,512]{1,0:T(8,128)(2,1)}, u32[]{:S(2)}) copy-start(bf16[3072,512]{1,0:T(8,128)(2,1)} %param.8) | copy-start | bytes 9437188
  44.2 1.9 %copy-start.6 = (bf16[3072,512]{1,0:T(8,128)(2,1)S(1)}, bf16[3072,512]{1,0:T(8,128)(2,1)}, u32[]{:S(2)}) copy-start(bf16[3072,512]{1,0:T(8,128)(2,1)} %param.7) | copy-start | bytes 9437188
  46.1 1.9 %copy-start.7 = (bf16[3072,512]{1,0:T(8,128)(2,1)S(1)}, bf16[3072,512]{1,0:T(8,128)(2,1)}, u32[]{:S(2)}) copy-start(bf16[3072,512]{1,0:T(8,128)(2,1)} %param.6) | copy-start | bytes 9437188
  50.0 1.2 copy-start.1
  51.4 11.7 %collective-permute-start = (f32[4,128,128]{2,1,0:T(8,128)S(1)}, f32[4,128,128]{2,1,0:T(8,128)S(1)}, u32[]{:S(2)}, u32[]{:S(2)}) collective-permute-start(f32[4,128,128]{2,1,0:T(8,128)S(1)} %fusion.2), channel_id=1, source_target_pairs={{0,8},{8,16},{16,24},{24,32},{32,40},{40,48},{48,56},{56,64},{64,7... | collective-permute-start | bytes 786440 | tf_op jit(solution)/shard_map/ppermute | solution.py:14
  63.1 11.1 %collective-permute-start.1 = (f32[4,128,128]{2,1,0:T(8,128)S(1)}, f32[4,128,128]{2,1,0:T(8,128)S(1)}, u32[]{:S(2)}, u32[]{:S(2)}) collective-permute-start(f32[4,128,128]{2,1,0:T(8,128)S(1)} %add.44), channel_id=1, source_target_pairs={{0,16},{8,24},{16,32},{24,40},{32,48},{40,56},{48,64},{56,72},{64,... | collective-permute-start | bytes 786440 | tf_op jit(solution)/shard_map/ppermute | solution.py:14
  74.3 24.9 %copy-start.2 = (f32[4,128,128]{2,1,0:T(8,128)}, f32[4,128,128]{2,1,0:T(8,128)S(1)}, u32[]{:S(2)}) copy-start(f32[4,128,128]{2,1,0:T(8,128)S(1)} %collective-permute-done.1) | copy-start | bytes 786436
  74.3 8.3 %collective-permute-start.2 = (f32[4,128,128]{2,1,0:T(8,128)S(1)}, f32[4,128,128]{2,1,0:T(8,128)S(1)}, u32[]{:S(2)}, u32[]{:S(2)}) collective-permute-start(f32[4,128,128]{2,1,0:T(8,128)S(1)} %add.46), channel_id=1, source_target_pairs={{0,32},{8,40},{16,48},{24,56},{32,64},{40,72},{48,80},{56,88},{64,... | collective-permute-start | bytes 786440 | tf_op jit(solution)/shard_map/ppermute | solution.py:14
  82.6 16.6 %copy-start.3 = (f32[4,128,128]{2,1,0:T(8,128)}, f32[4,128,128]{2,1,0:T(8,128)S(1)}, u32[]{:S(2)}) copy-start(f32[4,128,128]{2,1,0:T(8,128)S(1)} %collective-permute-done.2) | copy-start | bytes 786436
  82.6 15.7 %collective-permute-start.3 = (f32[4,128,128]{2,1,0:T(8,128)S(1)}, f32[4,128,128]{2,1,0:T(8,128)S(1)}, u32[]{:S(2)}, u32[]{:S(2)}) collective-permute-start(f32[4,128,128]{2,1,0:T(8,128)S(1)} %add.48), channel_id=1, source_target_pairs={{0,64},{8,72},{16,80},{24,88},{32,96},{40,104},{48,112},{56,120},{... | collective-permute-start | bytes 786440 | tf_op jit(solution)/shard_map/ppermute | solution.py:14
  98.3 0.8 copy-start.4
  99.1 18.4 %collective-permute-start.4 = (f32[4,128,128]{2,1,0:T(8,128)}, f32[4,128,128]{2,1,0:T(8,128)}, u32[]{:S(2)}, u32[]{:S(2)}) collective-permute-start(f32[4,128,128]{2,1,0:T(8,128)} %add.50), channel_id=1, source_target_pairs={{0,128},{8,136},{16,144},{24,152},{32,160},{40,168},{48,176},{56,1... | collective-permute-start | bytes 786440 | tf_op jit(solution)/shard_map/ppermute | solution.py:14
  104.2 15.8 %copy-start.5 = (f32[512]{0:T(512)S(1)}, f32[512]{0:T(512)}, u32[]{:S(2)}) copy-start(f32[512]{0:T(512)} %param.9) | copy-start | bytes 6148
